TPU v7x, 256 devices: a whole 4x4x8 slice. The times are simulated.
256 devices in a mesh: gx: 64 (over z, y, core), gy: 4 (over x).
Axes of the slice: x: 4, y: 4, z: 8, core: 2. Of those that a mesh axis runs over, the one named last changes fastest.
Arguments:
- embeds: bfloat16 [256, 2048, 768], P('gx', 'gy'), may hold values from -6 to 6
- fetch_list: int32 [2, 64, 64], replicated, may hold values from 0 to 16383, as said below
- partners: int32 [2, 64, 64, 2], replicated, may hold values from 0 to 255, as said below
- counts: int32 [256], replicated, may hold values from 512 to 2048
Outputs:
- nearest: float32 [256, 2048], P('gx', 'gy')
Inputs may be any that keep to these rules, and one draw needn't show every extreme that they name: fetch_list[w, h, g] // 64 is a block stored by index g of gx, that is g * 4 <= fetch_list[w, h, g] // 64 < (g + 1) * 4. partners[w, h, g, :] are 2 different blocks stored by index h of gx, none equal to fetch_list[w, h, g] // 64.
All inputs are finite; a program needn't handle non-finite values.
Results may differ from a plain program's by a relative error of at most 0.0003.
Values may be sent and summed in bfloat16 or wider, within the bound.
No kernel may reach another device: no remote copies, remote signals or barrier semaphores. Data moves between devices by JAX's collectives and lax.ppermute only.
A program may use at most 192 MiB of HBM per device.

v0:
```python
import jax
import jax.numpy as jnp
from jax import lax
from jax.sharding import PartitionSpec as P

SLICE = 8
EPS = 1e-06


def normalize(source):
    values = source.astype(jnp.float32)
    return (values * lax.rsqrt(jnp.sum(values * values, axis=-1, keepdims=True) + EPS)).astype(
        jnp.bfloat16
    )


def dense_tiles(arrived, row_valid, chosen, owned_full, col_valid):
    slots, lent_rows, width = arrived.shape
    owned, block, _ = owned_full.shape
    flat_rows = arrived.reshape(slots * lent_rows, width)
    listed = jnp.any(
        chosen[:, :, None] == jnp.arange(owned, dtype=jnp.int32)[None, None, :], axis=1
    )
    listed_pairs = jnp.transpose(listed.reshape(slots, owned // 2, 2), (1, 0, 2))
    column_pairs = owned_full.reshape(owned // 2, 2, block, width)
    valid_pairs = col_valid.reshape(owned // 2, 2, block)

    def advance(best_rows, entries):
        columns, picked, valid_cols = entries
        scores = jnp.einsum("rd,cbd->rcb", flat_rows, columns, preferred_element_type=jnp.float32)
        scores = scores.reshape(slots, lent_rows, 2, block)
        keep = row_valid[:, :, None, None] & picked[:, None, :, None] & valid_cols[None, None, :, :]
        scores = jnp.where(keep, scores, jnp.float32(-1.0))
        return (jnp.maximum(best_rows, jnp.max(scores, axis=(2, 3))), jnp.max(scores, axis=(0, 1)))

    start = jnp.full((slots, lent_rows), -1.0, jnp.float32)
    best_rows, col_parts = lax.scan(advance, start, (column_pairs, listed_pairs, valid_pairs))
    return (best_rows, col_parts.reshape(owned, block))


def on_device(embeds, fetch_list, partners, counts):
    owned, quarter, width = embeds.shape
    slice_rows = SLICE
    pieces = quarter // slice_rows
    my_group = lax.axis_index("gx")
    my_lane = lax.axis_index("gy")
    block = quarter * lax.axis_size("gy")
    first = my_group * owned
    waves = fetch_list.shape[0]
    own_unit = normalize(embeds)
    own_pieces = own_unit.reshape(owned, pieces, slice_rows, width)
    owned_full = lax.all_gather(own_unit, "gy", axis=1, tiled=True)
    positions = jnp.arange(block, dtype=jnp.int32)
    own_counts = lax.dynamic_slice_in_dim(counts, first, owned)
    col_valid = positions[None, :] < own_counts[:, None]
    row_positions = my_lane * quarter + jnp.arange(quarter, dtype=jnp.int32)
    slice_offsets = my_lane * quarter + jnp.arange(slice_rows, dtype=jnp.int32)
    local_ids = jnp.arange(owned, dtype=jnp.int32)
    piece_ids = jnp.arange(pieces, dtype=jnp.int32)
    row_total = jnp.full((owned, quarter), -1.0, jnp.float32)
    col_total = jnp.full((owned, block), -1.0, jnp.float32)
    for wave_index in range(waves):
        tiles = lax.dynamic_index_in_dim(fetch_list[wave_index], my_group, 1, False)
        outgoing_sent_block = tiles // pieces - first
        outgoing_sent_piece = tiles % pieces
        outbound = own_pieces[outgoing_sent_block, outgoing_sent_piece]
        arrived = lax.all_to_all(outbound, "gx", split_axis=0, concat_axis=0, tiled=True)
        incoming = lax.dynamic_index_in_dim(fetch_list[wave_index], my_group, 0, False)
        arrived_counts = counts[incoming // pieces]
        arrived_rows = (incoming % pieces)[:, None] * slice_rows + slice_offsets[None, :]
        row_valid = arrived_rows < arrived_counts[:, None]
        chosen = lax.dynamic_index_in_dim(partners[wave_index], my_group, 0, False) - first
        row_best, col_best = dense_tiles(arrived, row_valid, chosen, owned_full, col_valid)
        returned = lax.all_to_all(row_best, "gx", split_axis=0, concat_axis=0, tiled=True)
        match = (outgoing_sent_block[:, None, None] == local_ids[None, :, None]) & (
            outgoing_sent_piece[:, None, None] == piece_ids[None, None, :]
        )
        placed = jnp.max(
            jnp.where(match[:, :, :, None], returned[:, None, None, :], jnp.float32(-1.0)), axis=0
        )
        row_total = jnp.maximum(row_total, placed.reshape(owned, quarter))
        col_total = jnp.maximum(col_total, col_best)
    col_all = lax.pmax(col_total, "gy")
    col_mine = lax.dynamic_slice_in_dim(col_all, my_lane * quarter, quarter, 1)
    nearest = jnp.maximum(row_total, col_mine)
    mine_valid = row_positions[None, :] < own_counts[:, None]
    return jnp.where(mine_valid, nearest, jnp.float32(-1.0))


def solution(mesh):
    in_specs = (P("gx", "gy", None), P(), P(), P())
    out_specs = P("gx", "gy")
    return jax.shard_map(
        on_device, mesh=mesh, in_specs=in_specs, out_specs=out_specs, check_vma=False
    )
```

profile of v0, /device:TPU:1, one launch (start us, length us, event | category | flops | bytes accessed | tf_op | source)
XLA Modules:
  0.0 224.2 jit_solution(3750707437659595756)
XLA Ops:
  6.5 2.7 %fusion.18 = f32[4,512]{1,0:T(4,128)S(1)} fusion(bf16[4,512,768]{2,1,0:T(8,128)(2,1)} %param.8), kind=kLoop, calls=%fused_computation.36 | loop fusion | flops 4716544 | bytes 3153920 | tf_op jit(solution)/shard_map/reduce_sum | solution.py:12
  9.3 4.1 %fusion.19 = bf16[4,512,768]{2,1,0:T(8,128)(2,1)} fusion(bf16[4,512,768]{2,1,0:T(8,128)(2,1)} %param.8, f32[4,512]{1,0:T(4,128)S(1)} %add_rsqrt_fusion), kind=kLoop, calls=%fused_computation.37 | loop fusion | flops 4718592 | bytes 6299648 | tf_op jit(solution)/shard_map/convert_element_type | solution.py:12
  13.5 0.2 dynamic-slice_reduce_fusion
  13.7 2.2 %fusion.48 = bf16[4,64,8,768]{3,2,1,0:T(8,128)(2,1)} fusion(f32[4,512]{1,0:T(4,128)S(1)} %add_rsqrt_fusion, bf16[4,512,768]{2,1,0:T(8,128)(2,1)S(1)} %copy-done.1), kind=kLoop, calls=%fused_computation.135 | loop fusion | flops 4718592 | bytes 6299648 | tf_op jit(solution)/shard_map/reshape | solution.py:51
  16.0 3.5 %gather_fusion.3 = bf16[64,8,768]{2,1,0:T(8,128)(2,1)} fusion(bf16[4,64,8,768]{3,2,1,0:T(8,128)(2,1)} %fusion.48, s32[64]{0:T(128)S(1)} %fusion.42), kind=kCustom, calls=%fused_computation.3 | custom fusion | bytes 1573376 | tf_op jit(solution)/shard_map/gather | solution.py:66
  19.4 13.1 %all-to-all-start.2 = ((bf16[64,8,768]{2,1,0:T(8,128)(2,1)}), bf16[64,8,768]{2,1,0:T(8,128)(2,1)S(1)}, u32[]{:S(2)}, u32[]{:S(2)}) async-start(bf16[64,8,768]{2,1,0:T(8,128)(2,1)} %gather_fusion.3), calls=%async_computation.2 | async-start | bytes 1572864 | tf_op jit(solution)/shard_map/all_to_all | solution.py:67
  32.8 0.1 lt.161
  32.9 0.8 gather_fusion.2
  33.7 0.2 dynamic-slice_reduce_fusion.1
  33.9 3.7 %gather_fusion.1 = bf16[64,8,768]{2,1,0:T(8,128)(2,1)} fusion(bf16[4,64,8,768]{3,2,1,0:T(8,128)(2,1)} %fusion.48, s32[64]{0:T(128)S(1)} %fusion.43), kind=kCustom, calls=%fused_computation.1 | custom fusion | bytes 1573376 | tf_op jit(solution)/shard_map/gather | solution.py:66
  37.7 0.8 gather_fusion
  38.8 0.1 broadcast_and_fusion.2
  39.0 0.1 broadcast_and_fusion.3
  39.1 0.1 iota_compare_fusion.2
  39.2 16.4 %all-to-all-done.2 = bf16[64,8,768]{2,1,0:T(8,128)(2,1)S(1)} async-done(((bf16[64,8,768]{2,1,0:T(8,128)(2,1)}), bf16[64,8,768]{2,1,0:T(8,128)(2,1)S(1)}, u32[]{:S(2)}, u32[]{:S(2)}) %all-to-all-start.2) | async-done | bytes 786464 | tf_op jit(solution)/shard_map/all_to_all | solution.py:67
  55.6 5.9 %all-to-all-start = ((bf16[64,8,768]{2,1,0:T(8,128)(2,1)}), bf16[64,8,768]{2,1,0:T(8,128)(2,1)S(1)}, u32[]{:S(2)}, u32[]{:S(2)}) async-start(bf16[64,8,768]{2,1,0:T(8,128)(2,1)} %gather_fusion.1), calls=%async_computation | async-start | bytes 1572864 | tf_op jit(solution)/shard_map/all_to_all | solution.py:67
  61.5 76.8 %all-gather.2.cloned.1.call-done = bf16[4,2048,768]{2,1,0:T(8,128)(2,1)} async-done(((bf16[4,512,768]{2,1,0:T(8,128)(2,1)}), bf16[4,2048,768]{2,1,0:T(8,128)(2,1)}) %all-gather.2.cloned.1.call-update) | async-done | bytes 12582928 | tf_op jit(solution)/shard_map/all_gather | solution.py:52
  138.3 15.5 %while.27 = (s32[]{:T(128)}, f32[64,8]{1,0:T(8,128)}, f32[2,2,2048]{2,1,0:T(2,128)S(1)}, pred[2,64,2]{1,2,0:T(4,128)(4,1)S(1)}, pred[2,2,2048]{2,1,0:T(4,128)(4,...) while((s32[]{:T(128)}, f32[64,8]{1,0:T(8,128)}, ...), condition=%wide.region_11.12_spmd.clone, body=%wide.region_8.11_spmd.clone.sunk | while | flops 3229612544 | bytes 7160887 | solution.py:37
  138.5 0.1 and.440
  138.7 0.1 and.441
  138.8 6.2 %fusion.52 = (f32[2,2048]{1,0:T(2,128)S(1)}, f32[512]{0:T(512)S(1)}) fusion(pred[2,2048]{1,0:T(4,128)(4,1)S(1)} %dynamic-slice_bitcast_fusion.10, pred[512,2]{0,1:T(4,128)(4,1)S(1)} %broadcast_and_fusion.7, bf16[512,768]{1,0:T(8,128)(2,1)S(1)} %get-tuple-element.389, bf16[2,2,2048,768]{3,2,1,0:T(8,128)(2,1)} %get-tuple-element.388, s32[]{:T(128)S(6)} %copy.19), kind=kOutput, calls=%fused_computation.21.clone.1 | convolution fusion | flops 3229609472 | bytes 7101444 | tf_op jit(solution)/shard_map/while/body/eval_jaxpr/rd,cbd->rcb/dot_general | solution.py:30
  145.0 0.1 reduce_max.79
  145.1 0.6 select_maximum_fusion.5
  145.9 0.1 and.440
  146.1 0.1 and.441
  146.2 6.2 %fusion.52 = (f32[2,2048]{1,0:T(2,128)S(1)}, f32[512]{0:T(512)S(1)}) fusion(pred[2,2048]{1,0:T(4,128)(4,1)S(1)} %dynamic-slice_bitcast_fusion.10, pred[512,2]{0,1:T(4,128)(4,1)S(1)} %broadcast_and_fusion.7, bf16[512,768]{1,0:T(8,128)(2,1)S(1)} %get-tuple-element.389, bf16[2,2,2048,768]{3,2,1,0:T(8,128)(2,1)} %get-tuple-element.388, s32[]{:T(128)S(6)} %copy.19), kind=kOutput, calls=%fused_computation.21.clone.1 | convolution fusion | flops 3229609472 | bytes 7101444 | tf_op jit(solution)/shard_map/while/body/eval_jaxpr/rd,cbd->rcb/dot_general | solution.py:30
  152.4 0.1 reduce_max.79
  152.5 1.4 select_maximum_fusion.5
  153.9 10.9 %all-to-all-start.3 = ((f32[64,1,8]{2,1,0:T(1,128)}), f32[64,1,8]{2,1,0:T(1,128)S(1)}, u32[]{:S(2)}, u32[]{:S(2)}) async-start(f32[64,1,8]{2,1,0:T(1,128)} %bitcast.18), calls=%async_computation.3 | async-start | bytes 65536 | tf_op jit(solution)/shard_map/all_to_all | solution.py:74
  164.8 15.5 %while.26 = (s32[]{:T(128)}, f32[64,8]{1,0:T(8,128)}, f32[2,2,2048]{2,1,0:T(2,128)S(1)}, pred[2,64,2]{1,2,0:T(4,128)(4,1)S(1)}, pred[2,2,2048]{2,1,0:T(4,128)(4,...) while((s32[]{:T(128)}, f32[64,8]{1,0:T(8,128)}, ...), condition=%wide.region_5.6_spmd.clone, body=%wide.region_2.5_spmd.clone.sunk | while | flops 3229612544 | bytes 7160887 | solution.py:37
  164.9 0.1 and.432
  165.1 0.1 and.433
  165.2 6.2 %fusion.51 = (f32[2,2048]{1,0:T(2,128)S(1)}, f32[512]{0:T(512)S(1)}) fusion(pred[2,2048]{1,0:T(4,128)(4,1)S(1)} %dynamic-slice_bitcast_fusion.8, pred[512,2]{0,1:T(4,128)(4,1)S(1)} %broadcast_and_fusion.6, bf16[512,768]{1,0:T(8,128)(2,1)S(1)} %get-tuple-element.425, bf16[2,2,2048,768]{3,2,1,0:T(8,128)(2,1)} %get-tuple-element.424, s32[]{:T(128)S(6)} %copy.28), kind=kOutput, calls=%fused_computation.7.clone.1 | convolution fusion | flops 3229609472 | bytes 7101444 | tf_op jit(solution)/shard_map/while/body/eval_jaxpr/rd,cbd->rcb/dot_general | solution.py:30
  171.4 0.1 reduce_max.77
  171.5 0.6 select_maximum_fusion.4
  172.3 0.1 and.432
  172.5 0.1 and.433
  172.6 6.2 %fusion.51 = (f32[2,2048]{1,0:T(2,128)S(1)}, f32[512]{0:T(512)S(1)}) fusion(pred[2,2048]{1,0:T(4,128)(4,1)S(1)} %dynamic-slice_bitcast_fusion.8, pred[512,2]{0,1:T(4,128)(4,1)S(1)} %broadcast_and_fusion.6, bf16[512,768]{1,0:T(8,128)(2,1)S(1)} %get-tuple-element.425, bf16[2,2,2048,768]{3,2,1,0:T(8,128)(2,1)} %get-tuple-element.424, s32[]{:T(128)S(6)} %copy.28), kind=kOutput, calls=%fused_computation.7.clone.1 | convolution fusion | flops 3229609472 | bytes 7101444 | tf_op jit(solution)/shard_map/while/body/eval_jaxpr/rd,cbd->rcb/dot_general | solution.py:30
  178.8 0.1 reduce_max.77
  178.9 1.4 select_maximum_fusion.4
  180.4 12.3 %pmax.7 = f32[4,2048]{1,0:T(4,128)S(1)} all-reduce(f32[4,2048]{1,0:T(4,128)S(1)} %max.26), channel_id=1, replica_groups=mesh['gx'=64,'gy'=4] {'gy'}, use_global_device_ids=true, to_apply=%region_13.14 | all-reduce | flops 8192 | bytes 65536 | tf_op jit(solution)/shard_map/pmax | solution.py:83
  192.7 14.1 %all-to-all-start.1 = ((f32[64,1,8]{2,1,0:T(1,128)}), f32[64,1,8]{2,1,0:T(1,128)S(1)}, u32[]{:S(2)}, u32[]{:S(2)}) async-start(f32[64,1,8]{2,1,0:T(1,128)} %bitcast.9), calls=%async_computation.1 | async-start | bytes 65536 | tf_op jit(solution)/shard_map/all_to_all | solution.py:74
  206.8 0.2 select_reduce_fusion
  207.0 9.2 %all-to-all-done.1 = f32[64,1,8]{2,1,0:T(1,128)S(1)} async-done(((f32[64,1,8]{2,1,0:T(1,128)}), f32[64,1,8]{2,1,0:T(1,128)S(1)}, u32[]{:S(2)}, u32[]{:S(2)}) %all-to-all-start.1) | async-done | bytes 2080 | tf_op jit(solution)/shard_map/all_to_all | solution.py:74
  216.2 0.2 select_reduce_fusion.1
  216.4 0.1 copy.13
  216.5 0.1 max.24
  216.6 0.7 maximum_select_fusion
  (66 shorter events, 1.5 us)
Async XLA Ops:
  6.5 7.2 %copy-start.1 = (bf16[4,512,768]{2,1,0:T(8,128)(2,1)S(1)}, bf16[4,512,768]{2,1,0:T(8,128)(2,1)}, u32[]{:S(2)}) copy-start(bf16[4,512,768]{2,1,0:T(8,128)(2,1)} %param.8) | copy-start | bytes 9437188
  6.5 6.9 %copy-start.3 = (s32[2,64,64]{2,1,0:T(8,128)S(1)}, s32[2,64,64]{2,1,0:T(8,128)}, u32[]{:S(2)}) copy-start(s32[2,64,64]{2,1,0:T(8,128)} %param.9) | copy-start | bytes 98308
  6.5 131.8 %all-gather.2.cloned.1.call-start = ((), (), s32[]{:S(2)}) async-start(), calls=%async_computation.4 | async-start | bytes 15728640 | tf_op jit(solution)/shard_map/all_gather | solution.py:52
  13.4 19.2 %copy-start.2 = (s32[2,64,64,2]{2,3,1,0:T(2,128)S(1)}, s32[2,64,64,2]{2,3,1,0:T(2,128)}, u32[]{:S(2)}) copy-start(s32[2,64,64,2]{2,3,1,0:T(2,128)} %param.10) | copy-start | bytes 196612
  13.4 19.2 %copy-start = (s32[256]{0:T(256)S(1)}, s32[256]{0:T(256)}, u32[]{:S(2)}) copy-start(s32[256]{0:T(256)} %param.11) | copy-start | bytes 3076
  19.4 36.2 %all-to-all-start.2 = ((bf16[64,8,768]{2,1,0:T(8,128)(2,1)}), bf16[64,8,768]{2,1,0:T(8,128)(2,1)S(1)}, u32[]{:S(2)}, u32[]{:S(2)}) async-start(bf16[64,8,768]{2,1,0:T(8,128)(2,1)} %gather_fusion.3), calls=%async_computation.2 | async-start | bytes 1572864 | tf_op jit(solution)/shard_map/all_to_all | solution.py:67
  55.6 98.3 %all-to-all-start = ((bf16[64,8,768]{2,1,0:T(8,128)(2,1)}), bf16[64,8,768]{2,1,0:T(8,128)(2,1)S(1)}, u32[]{:S(2)}, u32[]{:S(2)}) async-start(bf16[64,8,768]{2,1,0:T(8,128)(2,1)} %gather_fusion.1), calls=%async_computation | async-start | bytes 1572864 | tf_op jit(solution)/shard_map/all_to_all | solution.py:67
  153.9 38.8 %all-to-all-start.3 = ((f32[64,1,8]{2,1,0:T(1,128)}), f32[64,1,8]{2,1,0:T(1,128)S(1)}, u32[]{:S(2)}, u32[]{:S(2)}) async-start(f32[64,1,8]{2,1,0:T(1,128)} %bitcast.18), calls=%async_computation.3 | async-start | bytes 65536 | tf_op jit(solution)/shard_map/all_to_all | solution.py:74
  192.7 23.5 %all-to-all-start.1 = ((f32[64,1,8]{2,1,0:T(1,128)}), f32[64,1,8]{2,1,0:T(1,128)S(1)}, u32[]{:S(2)}, u32[]{:S(2)}) async-start(f32[64,1,8]{2,1,0:T(1,128)} %bitcast.9), calls=%async_computation.1 | async-start | bytes 65536 | tf_op jit(solution)/shard_map/all_to_all | solution.py:74
Sparse Core Ops, SparseCore 0:
  13.6 124.6 all-gather.1
where the time goes:
time: 225 us; the launch traced here: 224 us
  waiting for transfers between devices  102 us (45%)
  starting transfers between devices  44 us (20%)
  matrix products  24.8 us (11%)
  other arithmetic  15.5 us (7%)
  between operations  13.7 us (6%)
  blocking collectives  12.3 us (5%)
  local copies, waits for them, and re-layouts  11.2 us (5%)
    all_gather x1, waiting for transfers between devices, on_device(): owned_full = lax.all_gather(own_unit, 'gy', axis=1, tiled=True)  76.8 us
    all_to_all x2, starting transfers between devices, on_device(): lax.all_to_all(row_best, 'gx', split_axis=0, concat_axis=0, tiled=True)  24.9 us
    dot_general x4, matrix products, advance(): jnp.einsum('rd,cbd->rcb', flat_rows, columns, preferred_element_type=jnp....  24.8 us
    all_to_all x2, starting transfers between devices, on_device(): lax.all_to_all(outbound, 'gx', split_axis=0, concat_axis=0, tiled=True)  19.1 us
    all_to_all x2, waiting for transfers between devices, on_device(): lax.all_to_all(outbound, 'gx', split_axis=0, concat_axis=0, tiled=True)  16.4 us
    pmax x1, blocking collectives, on_device(): col_all = lax.pmax(col_total, 'gy')  12.3 us
    all_to_all x2, waiting for transfers between devices, on_device(): lax.all_to_all(row_best, 'gx', split_axis=0, concat_axis=0, tiled=True)  9.17 us
    gather x2, local copies, waits for them, and re-layouts, on_device(): outbound = own_pieces[outgoing_sent_block, outgoing_sent_piece]  7.19 us
  transfers between devices with their start and end apart: 5, of which 3 were waited for; matrix products, arithmetic and copies ran while one was open for 19% of the time, Pallas kernels for 0%

commit v1 on v0

--- a/solution.py
+++ b/solution.py
@@ -5,6 +5,28 @@
 
 SLICE = 8
 EPS = 1e-06
+
+
+def joined_along(pieces, dim):
+    pieces = jnp.moveaxis(pieces, 0, dim)
+    lengths = pieces.shape
+    return pieces.reshape(*lengths[:dim], lengths[dim] * lengths[dim + 1], *lengths[dim + 2 :])
+
+
+def ring_gather(x, axis, dim):
+    devices = lax.axis_size(axis)
+    pairs = [(i, (i + 1) % devices) for i in range(devices)]
+    back = [(b, a) for a, b in pairs]
+    lower, upper = ([], [])
+    for step in range(devices - 1):
+        if step % 2 == 0:
+            lower.append(lax.ppermute(lower[-1] if lower else x, axis, pairs))
+        else:
+            upper.append(lax.ppermute(upper[-1] if upper else x, axis, back))
+    blocks = jnp.stack([*lower[::-1], x, *upper])
+    shift = lax.axis_index(axis) - len(lower)
+    blocks = blocks[(jnp.arange(devices) - shift) % devices]
+    return joined_along(blocks, dim)
 
 
 def normalize(source):
@@ -49,7 +71,7 @@
     waves = fetch_list.shape[0]
     own_unit = normalize(embeds)
     own_pieces = own_unit.reshape(owned, pieces, slice_rows, width)
-    owned_full = lax.all_gather(own_unit, "gy", axis=1, tiled=True)
+    owned_full = ring_gather(own_unit, "gy", 1)
     positions = jnp.arange(block, dtype=jnp.int32)
     own_counts = lax.dynamic_slice_in_dim(counts, first, owned)
     col_valid = positions[None, :] < own_counts[:, None]

time: 225 us -> 280 us (1.24)
  local copies, waits for them, and re-layouts: 11.2 us -> 36.3 us
  waiting for transfers between devices: 102 us -> 121 us
  other arithmetic: 15.5 us -> 29.6 us
  between operations: 13.7 us -> 0.33 us
  starting transfers between devices: 44 us -> 54.4 us
    ppermute x0 -> x3, waiting for transfers between devices: none -> 105 us  [the longest x2 105 us: ring_gather(): lower.append(lax.ppermute(lower[-1] if lower else x, axis, pairs))]
    all_gather x1 -> x0, waiting for transfers between devices: 76.8 us -> none  [on_device(): owned_full = lax.all_gather(own_unit, 'gy', axis=1, tiled=True)]
    gather x0 -> x3, local copies, waits for them, and re-layouts: none -> 19.4 us  [ring_gather(): blocks = blocks[(jnp.arange(devices) - shift) % devices]]
    all_to_all x2, starting transfers between devices: 19.1 us -> 29.8 us  [on_device(): lax.all_to_all(outbound, 'gx', split_axis=0, concat_axis=0, tiled=True)]
    all_to_all x2, waiting for transfers between devices: 16.4 us -> 7.06 us  [on_device(): lax.all_to_all(outbound, 'gx', split_axis=0, concat_axis=0, tiled=True)]
    another operation x0 -> x2, other arithmetic: none -> 6.23 us  [ring_gather(): blocks = jnp.stack([*lower[::-1], x, *upper])]
    transpose x0 -> x1, other arithmetic: none -> 6.19 us  [joined_along(): pieces = jnp.moveaxis(pieces, 0, dim)]
    all_to_all x2, starting transfers between devices: 24.9 us -> 19.3 us  [on_device(): lax.all_to_all(row_best, 'gx', split_axis=0, concat_axis=0, tiled=True)]
  transfers between devices with their start and end apart: 5 -> 7, of which waited for: 3 -> 4; matrix products, arithmetic and copies ran while one was open for 19% -> 24% of each run, Pallas kernels for 0% -> 0%
where the time goes in v1:
time: 280 us; the launch traced here: 279 us
  waiting for transfers between devices  121 us (43%)
  starting transfers between devices  54.4 us (19%)
  local copies, waits for them, and re-layouts  36.3 us (13%)
  other arithmetic  29.6 us (11%)
  matrix products  25.2 us (9%)
  blocking collectives  11.6 us (4%)
    ppermute x2, waiting for transfers between devices, ring_gather(): lower.append(lax.ppermute(lower[-1] if lower else x, axis, pairs))  105 us
    all_to_all x2, starting transfers between devices, on_device(): lax.all_to_all(outbound, 'gx', split_axis=0, concat_axis=0, tiled=True)  29.8 us
    dot_general x4, matrix products, advance(): jnp.einsum('rd,cbd->rcb', flat_rows, columns, preferred_element_type=jnp....  25.2 us
    gather x3, local copies, waits for them, and re-layouts, ring_gather(): blocks = blocks[(jnp.arange(devices) - shift) % devices]  19.4 us
    all_to_all x2, starting transfers between devices, on_device(): lax.all_to_all(row_best, 'gx', split_axis=0, concat_axis=0, tiled=True)  19.3 us
    pmax x1, blocking collectives, on_device(): col_all = lax.pmax(col_total, 'gy')  11.6 us
    all_to_all x2, waiting for transfers between devices, on_device(): lax.all_to_all(row_best, 'gx', split_axis=0, concat_axis=0, tiled=True)  9.16 us
    all_to_all x2, waiting for transfers between devices, on_device(): lax.all_to_all(outbound, 'gx', split_axis=0, concat_axis=0, tiled=True)  7.06 us
  transfers between devices with their start and end apart: 7, of which 4 were waited for; matrix products, arithmetic and copies ran while one was open for 24% of the time, Pallas kernels for 0%

profile of v1, /device:TPU:1, one launch (start us, length us, event | category | flops | bytes accessed | tf_op | source)
XLA Modules:
  0.0 278.8 jit_solution(9657387062562303953)
XLA Ops:
  0.0 2.7 fusion.18
  2.8 4.1 %fusion.19 = bf16[4,512,768]{2,1,0:T(8,128)(2,1)} fusion(bf16[4,512,768]{2,1,0:T(8,128)(2,1)} %param.8, f32[4,512]{1,0:T(4,128)S(1)} %add_rsqrt_fusion), kind=kLoop, calls=%fused_computation.41 | loop fusion | flops 4718592 | bytes 6299648 | tf_op jit(solution)/shard_map/convert_element_type | solution.py:34
  6.9 2.0 collective-permute-start
  8.9 1.3 collective-permute-start.2
  10.3 0.2 dynamic-slice_reduce_fusion.1
  10.5 2.2 fusion.51
  12.7 3.5 %gather_fusion.1 = bf16[64,8,768]{2,1,0:T(8,128)(2,1)} fusion(bf16[4,64,8,768]{3,2,1,0:T(8,128)(2,1)} %fusion.51, s32[64]{0:T(128)S(1)} %fusion.45), kind=kCustom, calls=%fused_computation.1 | custom fusion | bytes 1573376 | tf_op jit(solution)/shard_map/gather | solution.py:88
  16.2 13.2 %all-to-all-start = ((bf16[64,8,768]{2,1,0:T(8,128)(2,1)}), bf16[64,8,768]{2,1,0:T(8,128)(2,1)}, u32[]{:S(2)}, u32[]{:S(2)}) async-start(bf16[64,8,768]{2,1,0:T(8,128)(2,1)} %gather_fusion.1), calls=%async_computation | async-start | bytes 1572864 | tf_op jit(solution)/shard_map/all_to_all | solution.py:89
  29.6 0.5 copy-done.7
  30.1 0.8 gather_fusion
  30.9 0.2 dynamic-slice_reduce_fusion
  31.1 3.5 %gather_fusion.3 = bf16[64,8,768]{2,1,0:T(8,128)(2,1)} fusion(bf16[4,64,8,768]{3,2,1,0:T(8,128)(2,1)} %fusion.51, s32[64]{0:T(128)S(1)} %fusion.44), kind=kCustom, calls=%fused_computation.3 | custom fusion | bytes 1573376 | tf_op jit(solution)/shard_map/gather | solution.py:88
  34.6 41.5 %collective-permute-done = bf16[4,512,768]{2,1,0:T(8,128)(2,1)} collective-permute-done((bf16[4,512,768]{2,1,0:T(8,128)(2,1)}, bf16[4,512,768]{2,1,0:T(8,128)(2,1)}, u32[]{:S(2)}, u32[]{:S(2)}) %collective-permute-start) | collective-permute-done | bytes 3145760 | tf_op jit(solution)/shard_map/ppermute | solution.py:23
  76.1 1.9 collective-permute-start.1
  78.0 0.8 gather_fusion.2
  78.9 0.6 iota_add_fusion
  79.8 0.7 broadcast_and_fusion.3
  80.5 0.7 broadcast_and_fusion.2
  81.3 0.6 fusion.52
  82.0 63.3 %collective-permute-done.1 = bf16[4,512,768]{2,1,0:T(8,128)(2,1)} collective-permute-done((bf16[4,512,768]{2,1,0:T(8,128)(2,1)}, bf16[4,512,768]{2,1,0:T(8,128)(2,1)}, u32[]{:S(2)}, u32[]{:S(2)}) %collective-permute-start.1) | collective-permute-done | bytes 3145760 | tf_op jit(solution)/shard_map/ppermute | solution.py:23
  145.3 5.7 %pad_maximum_fusion = bf16[4,4,512,768]{3,2,1,0:T(8,128)(2,1)S(1)} fusion(bf16[1,4,512,768]{3,2,1,0:T(8,128)(2,1)} %bitcast.5, bf16[1,4,512,768]{3,2,1,0:T(8,128)(2,1)S(1)} %fusion.52, bf16[1,4,512,768]{3,2,1,0:T(8,128)(2,1)} %bitcast.3, bf16[1,4,512,768]{3,2,1,0:T(8,128)(2,1)} %bitcast.2), kind=kLoop, calls=%fused_computation.36 | loop fusion | flops 18874368 | bytes 25165824 | tf_op jit(solution)/shard_map/stack | solution.py:26
  150.9 5.6 %fusion.48 = (bf16[4,4,512,384]{3,2,1,0:T(8,128)(2,1)}, bf16[4,4,512,384]{3,2,1,0:T(8,128)(2,1)}) fusion(bf16[4,4,512,768]{3,2,1,0:T(8,128)(2,1)S(1)} %pad_maximum_fusion), kind=kLoop, calls=%fused_computation.144 | loop fusion | bytes 25165824 | tf_op jit(solution)/shard_map/gather | solution.py:28
  156.6 6.9 %gather_fusion.4 = bf16[4,4,512,384]{3,2,1,0:T(8,128)(2,1)} fusion(bf16[4,4,512,384]{3,2,1,0:T(8,128)(2,1)} %get-tuple-element.215, s32[1024]{0:T(1024)S(1)} %pad_clamp_fusion.2), kind=kCustom, calls=%fused_computation.4 | custom fusion | bytes 12582928 | tf_op jit(solution)/shard_map/gather | solution.py:28
  163.4 6.8 %gather_fusion.5 = bf16[4,4,512,384]{3,2,1,0:T(8,128)(2,1)} fusion(bf16[4,4,512,384]{3,2,1,0:T(8,128)(2,1)} %get-tuple-element.216, s32[1024]{0:T(1024)S(1)} %pad_clamp_fusion.2), kind=kCustom, calls=%fused_computation.5 | custom fusion | bytes 12582928 | tf_op jit(solution)/shard_map/gather | solution.py:28
  170.3 6.2 %maximum_bitcast_fusion = bf16[4,4,512,768]{3,2,0,1:T(8,128)(2,1)S(1)} fusion(bf16[4,4,512,384]{3,2,1,0:T(8,128)(2,1)} %gather_fusion.5, bf16[4,4,512,384]{3,2,1,0:T(8,128)(2,1)} %gather_fusion.4), kind=kLoop, calls=%fused_computation.37 | loop fusion | flops 25165824 | bytes 25165824 | tf_op jit(solution)/shard_map/transpose | solution.py:11
  176.5 5.5 %copy.16 = bf16[4,4,512,768]{3,2,1,0:T(8,128)(2,1)} copy(bf16[4,4,512,768]{3,2,0,1:T(8,128)(2,1)S(1)} %maximum_bitcast_fusion) | data formatting | bytes 25165824 | tf_op jit(solution)/shard_map/transpose | solution.py:11
  182.0 16.7 %all-to-all-start.2 = ((bf16[64,8,768]{2,1,0:T(8,128)(2,1)}), bf16[64,8,768]{2,1,0:T(8,128)(2,1)S(1)}, u32[]{:S(2)}, u32[]{:S(2)}) async-start(bf16[64,8,768]{2,1,0:T(8,128)(2,1)} %gather_fusion.3), calls=%async_computation.2 | async-start | bytes 1572864 | tf_op jit(solution)/shard_map/all_to_all | solution.py:89
  198.7 15.9 %while.26 = (s32[]{:T(128)}, f32[64,8]{1,0:T(8,128)}, f32[2,2,2048]{2,1,0:T(2,128)S(1)}, pred[2,64,2]{1,2,0:T(4,128)(4,1)S(1)}, pred[2,2,2048]{2,1,0:T(4,128)(4,...) while((s32[]{:T(128)}, f32[64,8]{1,0:T(8,128)}, ...), condition=%wide.region_5.6_spmd.clone, body=%wide.region_2.5_spmd.clone.sunk | while | flops 3229612544 | bytes 7161387 | solution.py:59
  198.8 0.1 and.456
  199.2 6.4 %fusion.55 = (f32[2,2048]{1,0:T(2,128)S(1)}, f32[512]{0:T(512)S(1)}) fusion(pred[2,2048]{1,0:T(4,128)(4,1)S(1)} %dynamic-slice_bitcast_fusion.8, pred[512,2]{0,1:T(4,128)(4,1)S(1)} %broadcast_and_fusion.6, bf16[512,768]{1,0:T(8,128)(2,1)} %get-tuple-element.427, bf16[2,2,2048,768]{3,2,1,0:T(8,128)(2,1)} %get-tuple-element.426, s32[]{:T(128)} %get-tuple-element.409), kind=kOutput, calls=%fused_computation.9.clone.1 | convolution fusion | flops 3229609472 | bytes 7101952 | tf_op jit(solution)/shard_map/while/body/eval_jaxpr/rd,cbd->rcb/dot_general | solution.py:52
  205.7 0.6 select_maximum_fusion.4
  206.4 0.1 and.456
  206.7 6.4 %fusion.55 = (f32[2,2048]{1,0:T(2,128)S(1)}, f32[512]{0:T(512)S(1)}) fusion(pred[2,2048]{1,0:T(4,128)(4,1)S(1)} %dynamic-slice_bitcast_fusion.8, pred[512,2]{0,1:T(4,128)(4,1)S(1)} %broadcast_and_fusion.6, bf16[512,768]{1,0:T(8,128)(2,1)} %get-tuple-element.427, bf16[2,2,2048,768]{3,2,1,0:T(8,128)(2,1)} %get-tuple-element.426, s32[]{:T(128)} %get-tuple-element.409), kind=kOutput, calls=%fused_computation.9.clone.1 | convolution fusion | flops 3229609472 | bytes 7101952 | tf_op jit(solution)/shard_map/while/body/eval_jaxpr/rd,cbd->rcb/dot_general | solution.py:52
  213.2 1.4 select_maximum_fusion.4
  214.6 7.1 %all-to-all-done.2 = bf16[64,8,768]{2,1,0:T(8,128)(2,1)S(1)} async-done(((bf16[64,8,768]{2,1,0:T(8,128)(2,1)}), bf16[64,8,768]{2,1,0:T(8,128)(2,1)S(1)}, u32[]{:S(2)}, u32[]{:S(2)}) %all-to-all-start.2) | async-done | bytes 786464 | tf_op jit(solution)/shard_map/all_to_all | solution.py:89
  221.7 15.5 %while.27 = (s32[]{:T(128)}, f32[64,8]{1,0:T(8,128)}, f32[2,2,2048]{2,1,0:T(2,128)S(1)}, pred[2,64,2]{1,2,0:T(4,128)(4,1)S(1)}, pred[2,2,2048]{2,1,0:T(4,128)(4,...) while((s32[]{:T(128)}, f32[64,8]{1,0:T(8,128)}, ...), condition=%wide.region_11.12_spmd.clone, body=%wide.region_8.11_spmd.clone.sunk | while | flops 3229612544 | bytes 7161387 | solution.py:59
  222.2 6.2 %fusion.56 = (f32[2,2048]{1,0:T(2,128)S(1)}, f32[512]{0:T(512)S(1)}) fusion(pred[2,2048]{1,0:T(4,128)(4,1)S(1)} %dynamic-slice_bitcast_fusion.10, pred[512,2]{0,1:T(4,128)(4,1)S(1)} %broadcast_and_fusion.7, bf16[512,768]{1,0:T(8,128)(2,1)S(1)} %get-tuple-element.391, bf16[2,2,2048,768]{3,2,1,0:T(8,128)(2,1)} %get-tuple-element.390, ...), kind=kOutput, calls=%fused_computation.23.clone.1 | convolution fusion | flops 3229609472 | bytes 7101952 | tf_op jit(solution)/shard_map/while/body/eval_jaxpr/rd,cbd->rcb/dot_general | solution.py:52
  228.5 0.6 select_maximum_fusion.5
  229.6 6.2 %fusion.56 = (f32[2,2048]{1,0:T(2,128)S(1)}, f32[512]{0:T(512)S(1)}) fusion(pred[2,2048]{1,0:T(4,128)(4,1)S(1)} %dynamic-slice_bitcast_fusion.10, pred[512,2]{0,1:T(4,128)(4,1)S(1)} %broadcast_and_fusion.7, bf16[512,768]{1,0:T(8,128)(2,1)S(1)} %get-tuple-element.391, bf16[2,2,2048,768]{3,2,1,0:T(8,128)(2,1)} %get-tuple-element.390, ...), kind=kOutput, calls=%fused_computation.23.clone.1 | convolution fusion | flops 3229609472 | bytes 7101952 | tf_op jit(solution)/shard_map/while/body/eval_jaxpr/rd,cbd->rcb/dot_general | solution.py:52
  235.9 1.4 select_maximum_fusion.5
  237.3 5.9 %all-to-all-start.1 = ((f32[64,1,8]{2,1,0:T(1,128)}), f32[64,1,8]{2,1,0:T(1,128)S(1)}, u32[]{:S(2)}, u32[]{:S(2)}) async-start(f32[64,1,8]{2,1,0:T(1,128)} %bitcast.15), calls=%async_computation.1 | async-start | bytes 65536 | tf_op jit(solution)/shard_map/all_to_all | solution.py:96
  243.2 11.6 %pmax.7 = f32[4,2048]{1,0:T(4,128)S(1)} all-reduce(f32[4,2048]{1,0:T(4,128)S(1)} %max.26), channel_id=1, replica_groups=mesh['gx'=64,'gy'=4] {'gy'}, use_global_device_ids=true, to_apply=%region_13.14 | all-reduce | flops 8192 | bytes 65536 | tf_op jit(solution)/shard_map/pmax | solution.py:105
  254.8 13.4 %all-to-all-start.3 = ((f32[64,1,8]{2,1,0:T(1,128)}), f32[64,1,8]{2,1,0:T(1,128)S(1)}, u32[]{:S(2)}, u32[]{:S(2)}) async-start(f32[64,1,8]{2,1,0:T(1,128)} %bitcast.24), calls=%async_computation.3 | async-start | bytes 65536 | tf_op jit(solution)/shard_map/all_to_all | solution.py:96
  268.2 0.2 select_reduce_fusion.1
  268.5 9.2 %all-to-all-done.3 = f32[64,1,8]{2,1,0:T(1,128)S(1)} async-done(((f32[64,1,8]{2,1,0:T(1,128)}), f32[64,1,8]{2,1,0:T(1,128)S(1)}, u32[]{:S(2)}, u32[]{:S(2)}) %all-to-all-start.3) | async-done | bytes 2080 | tf_op jit(solution)/shard_map/all_to_all | solution.py:96
  277.6 0.2 select_reduce_fusion
  278.0 0.1 max.24
  278.1 0.7 maximum_select_fusion
  (88 shorter events, 2.8 us)
Async XLA Ops:
  0.0 10.5 %copy-start.1 = (bf16[4,512,768]{2,1,0:T(8,128)(2,1)S(1)}, bf16[4,512,768]{2,1,0:T(8,128)(2,1)}, u32[]{:S(2)}) copy-start(bf16[4,512,768]{2,1,0:T(8,128)(2,1)} %param.8) | copy-start | bytes 9437188
  0.0 10.3 %copy-start.5 = (s32[2,64,64]{2,1,0:T(8,128)S(1)}, s32[2,64,64]{2,1,0:T(8,128)}, u32[]{:S(2)}) copy-start(s32[2,64,64]{2,1,0:T(8,128)} %param.9) | copy-start | bytes 98308
  6.9 22.5 %copy-start = (s32[256]{0:T(256)S(1)}, s32[256]{0:T(256)}, u32[]{:S(2)}) copy-start(s32[256]{0:T(256)} %param.11) | copy-start | bytes 3076
  6.9 22.7 %copy-start.2 = (s32[2,64,64,2]{2,3,1,0:T(2,128)S(1)}, s32[2,64,64,2]{2,3,1,0:T(2,128)}, u32[]{:S(2)}) copy-start(s32[2,64,64,2]{2,3,1,0:T(2,128)} %param.10) | copy-start | bytes 196612
  6.9 69.2 %collective-permute-start = (bf16[4,512,768]{2,1,0:T(8,128)(2,1)}, bf16[4,512,768]{2,1,0:T(8,128)(2,1)}, u32[]{:S(2)}, u32[]{:S(2)}) collective-permute-start(bf16[4,512,768]{2,1,0:T(8,128)(2,1)} %fusion.19), channel_id=1, source_target_pairs={{0,1},{1,2},{2,3},{3,0},{4,5},{5,6},{6,7},{7,4},{8,9},{9,10},{10,1... | collective-permute-start | bytes 9437192 | tf_op jit(solution)/shard_map/ppermute | solution.py:23
  8.9 73.0 %collective-permute-start.2 = (bf16[4,512,768]{2,1,0:T(8,128)(2,1)}, bf16[4,512,768]{2,1,0:T(8,128)(2,1)}, u32[]{:S(2)}, u32[]{:S(2)}) collective-permute-start(bf16[4,512,768]{2,1,0:T(8,128)(2,1)} %fusion.19), channel_id=1, source_target_pairs={{1,0},{2,1},{3,2},{0,3},{5,4},{6,5},{7,6},{4,7},{9,8},{10,9},{11,1... | collective-permute-start | bytes 9437192 | tf_op jit(solution)/shard_map/ppermute | solution.py:25
  16.2 165.8 %all-to-all-start = ((bf16[64,8,768]{2,1,0:T(8,128)(2,1)}), bf16[64,8,768]{2,1,0:T(8,128)(2,1)}, u32[]{:S(2)}, u32[]{:S(2)}) async-start(bf16[64,8,768]{2,1,0:T(8,128)(2,1)} %gather_fusion.1), calls=%async_computation | async-start | bytes 1572864 | tf_op jit(solution)/shard_map/all_to_all | solution.py:89
  29.5 0.6 copy-start.7
  76.1 69.1 %collective-permute-start.1 = (bf16[4,512,768]{2,1,0:T(8,128)(2,1)}, bf16[4,512,768]{2,1,0:T(8,128)(2,1)}, u32[]{:S(2)}, u32[]{:S(2)}) collective-permute-start(bf16[4,512,768]{2,1,0:T(8,128)(2,1)} %collective-permute-done), channel_id=1, source_target_pairs={{0,1},{1,2},{2,3},{3,0},{4,5},{5,6},{6,7},{7,4},{8,9},{9,10},{10,1... | collective-permute-start | bytes 9437192 | tf_op jit(solution)/shard_map/ppermute | solution.py:23
  182.0 39.7 %all-to-all-start.2 = ((bf16[64,8,768]{2,1,0:T(8,128)(2,1)}), bf16[64,8,768]{2,1,0:T(8,128)(2,1)S(1)}, u32[]{:S(2)}, u32[]{:S(2)}) async-start(bf16[64,8,768]{2,1,0:T(8,128)(2,1)} %gather_fusion.3), calls=%async_computation.2 | async-start | bytes 1572864 | tf_op jit(solution)/shard_map/all_to_all | solution.py:89
  221.7 46.5 %copy-start.4 = (pred[64,4,64]{2,1,0:T(4,128)(4,1)S(1)}, pred[64,4,64]{2,1,0:T(4,128)(4,1)}, u32[]{:S(2)}) copy-start(pred[64,4,64]{2,1,0:T(4,128)(4,1)} %broadcast_and_fusion.3) | copy-start | bytes 49156
  221.7 55.9 %copy-start.3 = (pred[64,4,64]{2,1,0:T(4,128)(4,1)S(1)}, pred[64,4,64]{2,1,0:T(4,128)(4,1)}, u32[]{:S(2)}) copy-start(pred[64,4,64]{2,1,0:T(4,128)(4,1)} %broadcast_and_fusion.2) | copy-start | bytes 49156
  221.7 56.4 %copy-start.6 = (s32[512]{0:T(512)S(1)}, s32[512]{0:T(512)}, u32[]{:S(2)}) copy-start(s32[512]{0:T(512)} %iota_add_fusion) | copy-start | bytes 6148
  221.7 56.4 %copy-start.8 = (s32[4]{0:T(128)S(1)}, s32[4]{0:T(128)}, u32[]{:S(2)}) copy-start(s32[4]{0:T(128)} %copy-done.7) | copy-start | bytes 52
  237.3 17.5 %all-to-all-start.1 = ((f32[64,1,8]{2,1,0:T(1,128)}), f32[64,1,8]{2,1,0:T(1,128)S(1)}, u32[]{:S(2)}, u32[]{:S(2)}) async-start(f32[64,1,8]{2,1,0:T(1,128)} %bitcast.15), calls=%async_computation.1 | async-start | bytes 65536 | tf_op jit(solution)/shard_map/all_to_all | solution.py:96
  254.8 22.8 %all-to-all-start.3 = ((f32[64,1,8]{2,1,0:T(1,128)}), f32[64,1,8]{2,1,0:T(1,128)S(1)}, u32[]{:S(2)}, u32[]{:S(2)}) async-start(f32[64,1,8]{2,1,0:T(1,128)} %bitcast.24), calls=%async_computation.3 | async-start | bytes 65536 | tf_op jit(solution)/shard_map/all_to_all | solution.py:96
